TPU v7x, 32 devices: a whole 2x2x4 slice. The times are simulated.
32 devices in a mesh: sky: 8 (over z, x), visit: 4 (over y, core).
Axes of the slice: x: 2, y: 2, z: 4, core: 2. Of those that a mesh axis runs over, the one named last changes fastest.
Arguments:
- tile_image: bfloat16 [4, 256, 128, 128], P('visit', 'sky'), may hold values from -1.1953125 to 1.1953125
- tile_variance: bfloat16 [4, 256, 128, 128], P('visit', 'sky'), may hold values from 0.099609375 to 10
- match_coeffs: bfloat16 [4, 256, 9], P('visit', 'sky'), may hold values from 0.25 to 9
- tile_patch: int32 [4, 256, 1], P('visit', 'sky'), may hold values from 0 to 7; in each aligned block of 32 rows (0 to 31, 32 to 63, ..., all dimensions but the last counted through in order) at most 8 rows name the same one
- tile_offset: int32 [4, 256], P('visit', 'sky'), may hold values from 0 to 63
- row_taps: bfloat16 [9, 41], replicated, may hold values from -1.1953125 to 1.1953125
- col_taps: bfloat16 [9, 41], replicated, may hold values from -1.1953125 to 1.1953125
Outputs:
- coadd_image: float32 [8192, 1024], P('sky', 'visit')
- coadd_variance: float32 [8192, 1024], P('sky', 'visit')
- coadd_psf: float32 [8, 41, 41], P('sky')
Inputs may be any that keep to these rules, and one draw needn't show every extreme that they name: `tile_patch`: among the 32 tiles of one device, at most 8 intersect any one patch.
All inputs are finite; a program needn't handle non-finite values.
Results may differ from a plain program's by a relative error of at most 0.0029.
Values may be sent and summed in bfloat16 or wider, within the bound.
No kernel may reach another device: no remote copies, remote signals or barrier semaphores. Data moves between devices by JAX's collectives and lax.ppermute only.
A program may use at most 64 MiB of HBM per device.

v0:
```python
import functools

import jax
import jax.numpy as jnp
from jax import lax
from jax.experimental import pallas as pl
from jax.experimental.pallas import tpu as pltpu
from jax.sharding import PartitionSpec as P

GRID = 8
BASIS = 9
META = 16
EXTRA = 8


weight_floor = 0.5


def band_table(taps, tile):
    span = taps.shape[1]
    offset = jnp.arange(tile)[:, None] - jnp.arange(tile)[None, :] + (span - 1) // 2
    select = (offset[None, :, :] == jnp.arange(span)[:, None, None]).astype(jnp.float32)
    return jnp.einsum("kt,tij->kij", taps.astype(jnp.float32), select).astype(jnp.bfloat16)


def place_tile(out_ref, row, group, sub, contrib):
    tile = contrib.shape[0]
    per_dev = out_ref.shape[2] // tile
    start = pl.multiple_of(row * tile, tile)
    for c in range(per_dev):

        @pl.when(sub == c)
        def _():
            out_ref[group, pl.ds(start, tile), c * tile:(c + 1) * tile] += contrib


def variance_kernel(row_ref, group_ref, sub_ref, w2_ref, *refs):
    chunks, extra_ref, out_ref = refs[:-2], refs[-2], refs[-1]
    held = chunks[0].shape[0]
    tile = chunks[0].shape[2]
    body_rows = out_ref.shape[1] - extra_ref.shape[1]
    out_ref[:, :body_rows, :] = jnp.zeros((out_ref.shape[0], body_rows, out_ref.shape[2]), jnp.float32)
    out_ref[:, body_rows:, :] = extra_ref[...]
    for d, chunk in enumerate(chunks):

        def body(r, carry):
            t = d * held + r
            row = row_ref[t]

            @pl.when(row >= 0)
            def _():
                contrib = w2_ref[t] * chunk[r, :tile, :].astype(jnp.float32)
                place_tile(out_ref, row, group_ref[t], sub_ref[t], contrib)

            return carry

        lax.fori_loop(0, held, body, 0)


def image_kernel(accumulate, order_ref, count_ref, row_ref, group_ref, sub_ref, w_ref, coef_ref,
                 img_ref, row_side_ref, col_side_ref, *refs):
    tile = img_ref.shape[2]
    out_ref = refs[-1]
    if accumulate:
        out_ref[...] = refs[0][...]
    else:
        out_ref[...] = jnp.zeros(out_ref.shape, jnp.float32)

    def body(p, carry):
        pair = (order_ref[2 * p], order_ref[2 * p + 1])
        both = jnp.concatenate([img_ref[pair[0]], img_ref[pair[1]]], axis=0)
        first = jnp.dot(both, row_side_ref[...], preferred_element_type=jnp.float32)
        blocks = []
        for k in range(BASIS):
            halves = [
                (first[h * tile:(h + 1) * tile, k * tile:(k + 1) * tile]
                 * coef_ref[pair[h] * BASIS + k]).astype(jnp.bfloat16)
                for h in range(2)
            ]
            blocks.append(jnp.concatenate(halves, axis=1))
        scaled = jnp.concatenate(blocks, axis=0)
        matched = jnp.dot(col_side_ref[...], scaled, preferred_element_type=jnp.float32)
        for h in range(2):
            t = pair[h]
            row = row_ref[t]

            @pl.when(row >= 0)
            def _():
                place_tile(out_ref, row, group_ref[t], sub_ref[t],
                           w_ref[t] * matched[:, h * tile:(h + 1) * tile])

        return carry

    lax.fori_loop(0, (count_ref[0] + 1) // 2, body, 0)


def smem():
    return pl.BlockSpec(memory_space=pltpu.SMEM)


def vmem():
    return pl.BlockSpec(memory_space=pltpu.VMEM)


def variance_field(where, w2, chunks, extra, field_shape):
    return pl.pallas_call(
        variance_kernel,
        out_shape=jax.ShapeDtypeStruct(field_shape, jnp.float32),
        in_specs=[smem()] * 4 + [vmem()] * (len(chunks) + 1),
        out_specs=vmem(),
    )(*where, w2, *chunks, extra)


def image_field(where, w, coef, images, row_side, col_side, field_shape, field=None):
    filled = where[0] >= 0
    order = jnp.argsort(jnp.logical_not(filled), stable=True).astype(jnp.int32)
    count = jnp.sum(filled.astype(jnp.int32))[None]
    args = [order, count, *where, w, coef, images, row_side, col_side]
    if field is not None:
        args.append(field)
    return pl.pallas_call(
        functools.partial(image_kernel, field is not None),
        out_shape=jax.ShapeDtypeStruct(field_shape, jnp.float32),
        in_specs=[smem()] * 7 + [vmem()] * (len(args) - 7),
        out_specs=vmem(),
        input_output_aliases={} if field is None else {len(args) - 1: 0},
        cost_estimate=pl.CostEstimate(
            flops=4 * images.shape[0] * images.shape[2] ** 3 * BASIS,
            transcendentals=0,
            bytes_accessed=images.size * 2 + 8 * (field_shape[0] * field_shape[1] * field_shape[2]),
        ),
    )(*args)


def split_exact(value):
    high = lax.reduce_precision(value, exponent_bits=8, mantissa_bits=7)
    rest = value - high
    middle = lax.reduce_precision(rest, exponent_bits=8, mantissa_bits=7)
    low = rest - middle
    return tuple(part.astype(jnp.bfloat16) for part in (high, middle, low))


def bit_reverse(values, bits):
    out = jnp.zeros_like(values)
    for b in range(bits):
        out = out | (((values >> b) & 1) << (bits - 1 - b))
    return out


def reduce_scatter_visit(field, n_visit):
    bits = n_visit.bit_length() - 1
    for b in range(bits):
        half = field.shape[0] // 2
        pairs = [(i, i ^ (1 << b)) for i in range(n_visit)]
        field = field[:half] + lax.ppermute(field[half:], "visit", perm=pairs)
    return field[0]


def shards(tile_image, tile_variance, match_coeffs, tile_patch, tile_offset, row_taps, col_taps):
    n_sky = lax.axis_size("sky")
    n_visit = lax.axis_size("visit")
    images = tile_image[0]
    variance = tile_variance[0]
    coeffs = match_coeffs[0]
    count = images.shape[0]
    tile = images.shape[1]
    held_most = max(2, 2 * count // n_sky)
    positions = GRID * GRID
    per_dev = GRID // n_visit
    dest = tile_patch[0, :, 0]
    offsets = tile_offset[0]
    band_row = band_table(row_taps, tile)
    band_col = band_table(col_taps, tile)
    row_side = band_row.transpose(1, 0, 2).reshape(tile, BASIS * tile)
    col_side = band_col.transpose(2, 0, 1).reshape(tile, BASIS * tile)
    order = jnp.arange(count)
    earlier = (dest[:, None] == dest[None, :]) & (order[None, :] < order[:, None])
    rank = jnp.sum(earlier.astype(jnp.int32), axis=1)
    slot = dest * held_most + rank
    slots_all = n_sky * held_most
    pick = (jnp.arange(slots_all)[:, None] == slot[None, :]).astype(jnp.bfloat16)
    me = lax.axis_index("sky")
    shift = (dest - me) % n_sky
    pick_shift = (jnp.arange(slots_all)[:, None] == (shift * held_most + rank)[None, :])
    weight_src = 1.0 / jnp.mean(variance.astype(jnp.float32), axis=(1, 2))
    w_parts = split_exact(weight_src)
    meta_row = jnp.concatenate(
        [coeffs, (offsets + 1).astype(jnp.bfloat16)[:, None]]
        + [part[:, None] for part in w_parts]
        + [jnp.zeros((count, tile - BASIS - 4), jnp.bfloat16)],
        axis=1,
    )
    meta = jnp.concatenate(
        [meta_row[:, None, :], jnp.zeros((count, META - 1, tile), jnp.bfloat16)], axis=1
    )
    var_meta = jnp.concatenate([variance, meta], axis=1)
    send_vm = jnp.dot(
        pick_shift.astype(jnp.bfloat16), var_meta.reshape(count, (tile + META) * tile),
        preferred_element_type=jnp.float32,
    )
    send_vm = send_vm.astype(jnp.bfloat16).reshape(n_sky, held_most, tile + META, tile)
    send_im = jnp.dot(
        pick, images.reshape(count, tile * tile), preferred_element_type=jnp.float32
    )
    send_im = send_im.astype(jnp.bfloat16).reshape(n_sky, held_most, tile, tile)

    got_vm = [send_vm[0]]
    for step in range(1, n_sky):
        pairs = [(src, (src + step) % n_sky) for src in range(n_sky)]
        got_vm.append(lax.ppermute(send_vm[step], "sky", perm=pairs))
    got_vm, send_im = lax.optimization_barrier((got_vm, send_im))
    got_meta = jnp.concatenate([chunk[:, tile, :] for chunk in got_vm]).astype(jnp.float32)
    got_coef = got_meta[:, :BASIS]
    place = got_meta[:, BASIS].astype(jnp.int32) - 1
    valid = place >= 0
    weight = (got_meta[:, BASIS + 1] + got_meta[:, BASIS + 2]) + got_meta[:, BASIS + 3]
    weight = jnp.where(valid, weight, 0.0)
    tile_row = jnp.where(valid, place // GRID, -1)
    tile_col = place % GRID
    bits = n_visit.bit_length() - 1
    me_visit = lax.axis_index("visit")
    where = (tile_row, bit_reverse((tile_col // per_dev) ^ me_visit, bits), tile_col % per_dev)
    psf_part = jnp.sum(weight[:, None] * got_coef, axis=0)
    weight_part = jnp.sum(weight)
    weight_pos = jnp.sum(
        jnp.where(jnp.arange(positions)[:, None] == place[None, :], weight[None, :], 0.0), axis=1
    )
    pos_lanes = weight_pos.reshape(GRID, n_visit, per_dev).transpose(1, 2, 0)
    pos_lanes = jnp.take(pos_lanes, bit_reverse(jnp.arange(n_visit), bits) ^ me_visit, axis=0)
    pos_lanes = jnp.concatenate(
        [pos_lanes, jnp.zeros((n_visit, per_dev, tile - GRID), jnp.float32)], axis=2
    ).reshape(n_visit, 1, per_dev * tile)
    psf_row = jnp.concatenate(
        [psf_part, weight_part[None], jnp.zeros((per_dev * tile - BASIS - 1,), jnp.float32)]
    )
    extra = jnp.concatenate(
        [
            pos_lanes,
            jnp.broadcast_to(psf_row[None, None, :], (n_visit, 1, per_dev * tile)),
            jnp.zeros((n_visit, EXTRA - 2, per_dev * tile), jnp.float32),
        ],
        axis=1,
    )
    var_pos = variance_field(
        where, weight * weight, got_vm, extra, (n_visit, GRID * tile + EXTRA, per_dev * tile)
    )
    var_share = reduce_scatter_visit(var_pos, n_visit)

    low = held_most // 2
    part_a = lax.all_to_all(send_im[:, :low], "sky", split_axis=0, concat_axis=0, tiled=True)
    var_share, part_a, send_b = lax.optimization_barrier((var_share, part_a, send_im[:, low:]))
    part_b = lax.all_to_all(send_b, "sky", split_axis=0, concat_axis=0, tiled=True)
    source = (me - jnp.arange(n_sky)) % n_sky

    def by_source(values, lower, upper):
        values = jnp.take(values.reshape(n_sky, held_most, -1), source, axis=0)
        return values[:, lower:upper].reshape(n_sky * (upper - lower), -1)

    field_shape = (n_visit, GRID * tile, per_dev * tile)
    image_pos = None
    for lower, upper, part in ((0, low, part_a), (low, held_most, part_b)):
        image_pos = image_field(
            tuple(by_source(values, lower, upper)[:, 0] for values in where),
            by_source(weight, lower, upper)[:, 0],
            by_source(got_coef, lower, upper).reshape(-1),
            part.reshape(n_sky * (upper - lower), tile, tile),
            row_side, col_side, field_shape, image_pos,
        )
    image_share = reduce_scatter_visit(image_pos, n_visit)

    body_rows = GRID * tile
    pos_weight = var_share[body_rows, :].reshape(per_dev, tile)[:, :GRID]
    denom = jnp.maximum(pos_weight, weight_floor).T
    denom = jnp.broadcast_to(denom[:, None, :, None], (GRID, tile, per_dev, tile))
    denom = denom.reshape(body_rows, per_dev * tile)
    coadd_image = image_share / denom
    coadd_variance = var_share[:body_rows, :] / (denom * denom)

    psf_total = var_share[body_rows + 1, :BASIS]
    weight_total = var_share[body_rows + 1, BASIS]
    share = psf_total / weight_total
    high = lax.Precision.HIGHEST
    coadd_psf = jnp.einsum(
        "k,ka,kb->ab",
        share,
        col_taps.astype(jnp.float32),
        row_taps.astype(jnp.float32),
        precision=high,
    )[None]
    return (coadd_image, coadd_variance, coadd_psf)


def solution(mesh):
    return jax.shard_map(
        shards,
        mesh=mesh,
        in_specs=(
            P("visit", "sky", None, None),
            P("visit", "sky", None, None),
            P("visit", "sky", None),
            P("visit", "sky", None),
            P("visit", "sky"),
            P(),
            P(),
        ),
        out_specs=(P("sky", "visit"), P("sky", "visit"), P("sky", None, None)),
        check_vma=False,
    )
```

profile of v0, /device:TPU:10, one launch (start us, length us, event | category | flops | bytes accessed | tf_op | source)
XLA Modules:
  0.0 204.9 jit_solution(17462381802896342214)
XLA Ops:
  0.6 1.6 convert_reduce_fusion
  5.9 1.5 maximum_maximum_fusion
  9.1 1.5 collective-permute-start
  11.4 1.6 collective-permute-start.1
  15.6 1.7 collective-permute-start.3
  18.1 1.3 collective-permute-start.4
  20.9 1.2 collective-permute-start.5
  22.1 27.8 %collective-permute-done.1.refs_2_ = bf16[8,144,128]{2,1,0:T(8,128)(2,1)S(1)} collective-permute-done((bf16[8,144,128]{2,1,0:T(8,128)(2,1)}, bf16[8,144,128]{2,1,0:T(8,128)(2,1)S(1)}, u32[]{:S(2)}, u32[]{:S(2)}) %collective-permute-start.1) | collective-permute-done | bytes 294944 | tf_op jit(solution)/shard_map/ppermute | solution.py:210
  51.5 4.8 %collective-permute-done.2.refs_3_ = bf16[8,144,128]{2,1,0:T(8,128)(2,1)} collective-permute-done((bf16[8,144,128]{2,1,0:T(8,128)(2,1)}, bf16[8,144,128]{2,1,0:T(8,128)(2,1)}, u32[]{:S(2)}, u32[]{:S(2)}) %collective-permute-start.2) | collective-permute-done | bytes 294944 | tf_op jit(solution)/shard_map/ppermute | solution.py:210
  56.3 5.2 %collective-permute-done.3.refs_4_ = bf16[8,144,128]{2,1,0:T(8,128)(2,1)} collective-permute-done((bf16[8,144,128]{2,1,0:T(8,128)(2,1)}, bf16[8,144,128]{2,1,0:T(8,128)(2,1)}, u32[]{:S(2)}, u32[]{:S(2)}) %collective-permute-start.3) | collective-permute-done | bytes 294944 | tf_op jit(solution)/shard_map/ppermute | solution.py:210
  61.5 1.8 collective-permute-done.5.refs_6_
  63.2 1.9 collective-permute-done.6.refs_7_
  74.1 5.7 %shard_map.94 = f32[4,1032,256]{2,1,0:T(8,128)} custom-call(s32[64]{0:T(128)} %get-tuple-element.105.row_ref, s32[64]{0:T(128)} %get-tuple-element.104.group_ref, s32[64]{0:T(128)} %get-tuple-element.70.sub_ref, f32[64]{0:T(128)} %mul.32.w2_ref, bf16[8,144,128]{2,1,0:T(8,128)(2,1)} %bitcast.165, bf16[8,144,128]{2,1,0:T(8,128)(2,1)} %copy-done.6, ...), custom_call_target="tpu_custom_call" | custom-call | tf_op jit(solution)/shard_map/pallas_call | solution.py:106
  79.8 3.1 %slice.219 = f32[2,1032,256]{2,1,0:T(8,128)} slice(f32[4,1032,256]{2,1,0:T(8,128)} %shard_map.94), slice={[2:4], [0:1032], [0:256]} | slice | bytes 4227072 | tf_op jit(solution)/shard_map/slice | solution.py:155
  82.9 1.5 fusion.8
  85.0 1.5 fusion.54
  86.4 4.9 %all-to-all-start = ((bf16[8,4,128,128]{3,2,1,0:T(8,128)(2,1)}), bf16[8,4,128,128]{3,2,1,0:T(8,128)(2,1)}, u32[]{:S(2)}, u32[]{:S(2)}) async-start(bf16[8,4,128,128]{3,2,1,0:T(8,128)(2,1)} %get-tuple-element.84), calls=%async_computation | async-start | bytes 2097152 | tf_op jit(solution)/shard_map/all_to_all | solution.py:250
  91.3 2.5 %slice_add_fusion = f32[2,1032,256]{2,1,0:T(8,128)S(1)} fusion(f32[2,1032,256]{2,1,0:T(8,128)} %collective-permute-done.7, f32[4,1032,256]{2,1,0:T(8,128)} %shard_map.94), kind=kLoop, calls=%fused_computation.11 | loop fusion | flops 528384 | bytes 6340608 | tf_op jit(solution)/shard_map/add | solution.py:155
  94.9 1.6 collective-permute-start.8
  96.5 1.5 fusion.7
  104.0 16.4 %collective-permute-done.8 = f32[1,1032,256]{2,1,0:T(8,128)} collective-permute-done((f32[1,1032,256]{2,1,0:T(8,128)}, f32[1,1032,256]{2,1,0:T(8,128)}, u32[]{:S(2)}, u32[]{:S(2)}) %collective-permute-start.8) | collective-permute-done | bytes 1056800 | tf_op jit(solution)/shard_map/ppermute | solution.py:155
  120.4 1.4 fusion.11
  121.8 6.0 %all-to-all-start.1 = ((bf16[8,4,128,128]{3,2,1,0:T(8,128)(2,1)}), bf16[8,4,128,128]{3,2,1,0:T(8,128)(2,1)S(1)}, u32[]{:S(2)}, u32[]{:S(2)}) async-start(bf16[8,4,128,128]{3,2,1,0:T(8,128)(2,1)} %get-tuple-element.30), calls=%async_computation.1 | async-start | bytes 2097152 | tf_op jit(solution)/shard_map/all_to_all | solution.py:252
  134.7 1.7 sort.32
  136.3 1.6 sort.31
  137.9 14.2 %shard_map.95.refs_0_ = f32[4,1024,256]{2,1,0:T(8,128)} custom-call(s32[32]{0:T(128)} %get-tuple-element.31.order_ref, s32[1]{0:T(128)} %bitcast.29.count_ref, s32[32]{0:T(128)} %copy-done.11, s32[32]{0:T(128)} %squeeze_reshape.29.group_ref, s32[32]{0:T(128)} %squeeze_reshape.30.sub_ref, f32[32]{0:T(128)} %squeeze_reshape.31.w_ref, ...), custom_call_target="tpu_custom_call" | custom-call | flops 2415919104 | bytes 9437184 | tf_op jit(solution)/shard_map/pallas_call | solution.py:121
  153.1 15.5 %shard_map.96 = f32[4,1024,256]{2,1,0:T(8,128)} custom-call(s32[32]{0:T(128)} %get-tuple-element.28.order_ref, s32[1]{0:T(128)} %bitcast.9.count_ref, s32[32]{0:T(128)} %copy-done.10, s32[32]{0:T(128)} %squeeze_reshape.25.group_ref, s32[32]{0:T(128)} %squeeze_reshape.26.sub_ref, f32[32]{0:T(128)} %squeeze_reshape.27.w_ref, ...), custom_call_target="tpu_custom_call", output_to_operand_aliasing={{}: (10, {})} | custom-call | flops 2415919104 | bytes 9437184 | tf_op jit(solution)/shard_map/pallas_call | solution.py:121
  168.7 1.9 slice.226
  170.6 4.1 %collective-permute-done.9 = f32[2,1024,256]{2,1,0:T(8,128)S(1)} collective-permute-done((f32[2,1024,256]{2,1,0:T(8,128)S(1)}, f32[2,1024,256]{2,1,0:T(8,128)S(1)}, u32[]{:S(2)}, u32[]{:S(2)}) %collective-permute-start.9) | collective-permute-done | bytes 2097184 | tf_op jit(solution)/shard_map/ppermute | solution.py:155
  176.1 1.6 collective-permute-start.10
  179.9 21.7 %collective-permute-done.10 = f32[1,1024,256]{2,1,0:T(8,128)} collective-permute-done((f32[1,1024,256]{2,1,0:T(8,128)}, f32[1,1024,256]{2,1,0:T(8,128)}, u32[]{:S(2)}, u32[]{:S(2)}) %collective-permute-start.10) | collective-permute-done | bytes 1048608 | tf_op jit(solution)/shard_map/ppermute | solution.py:155
  201.9 3.0 %fusion.12 = (f32[1024,256]{1,0:T(8,128)}, f32[1024,256]{1,0:T(8,128)}) fusion(f32[1032,256]{1,0:T(8,128)S(1)} %fusion.11, f32[128,8,2,128]{3,2,1,0:T(2,128)S(1)} %bitcast.163, f32[1,1024,256]{2,1,0:T(8,128)} %collective-permute-done.10, f32[2,1024,256]{2,1,0:T(8,128)S(1)} %slice_add_fusion.1), kind=kLoop, calls=%fused_computation.29 | loop fusion | flops 1048576 | bytes 6291456 | tf_op jit(solution)/shard_map/div | solution.py:277
  (150 shorter events, 40.7 us)
Async XLA Ops:
  0.6 82.3 %copy-start = (bf16[9,41]{1,0:T(8,128)(2,1)S(1)}, bf16[9,41]{1,0:T(8,128)(2,1)}, u32[]{:S(2)}) copy-start(bf16[9,41]{1,0:T(8,128)(2,1)} %param.18) | copy-start | bytes 2218
  9.1 41.6 %copy-start.4 = (bf16[1,32,128,128]{3,2,1,0:T(8,128)(2,1)S(1)}, bf16[1,32,128,128]{3,2,1,0:T(8,128)(2,1)}, u32[]{:S(2)}) copy-start(bf16[1,32,128,128]{3,2,1,0:T(8,128)(2,1)} %param.13) | copy-start | bytes 3145732
  9.1 11.8 %collective-permute-start = (bf16[8,144,128]{2,1,0:T(8,128)(2,1)}, bf16[8,144,128]{2,1,0:T(8,128)(2,1)S(1)}, u32[]{:S(2)}, u32[]{:S(2)}) collective-permute-start(bf16[8,144,128]{2,1,0:T(8,128)(2,1)} %bitcast.158), channel_id=1, source_target_pairs={{0,4},{4,8},{8,12},{12,16},{16,20},{20,24},{24,28},{28,0},{1,5},{5... | collective-permute-start | bytes 884744 | tf_op jit(solution)/shard_map/ppermute | solution.py:210
  11.4 38.6 %collective-permute-start.1 = (bf16[8,144,128]{2,1,0:T(8,128)(2,1)}, bf16[8,144,128]{2,1,0:T(8,128)(2,1)S(1)}, u32[]{:S(2)}, u32[]{:S(2)}) collective-permute-start(bf16[8,144,128]{2,1,0:T(8,128)(2,1)} %bitcast.157), channel_id=1, source_target_pairs={{0,8},{4,12},{8,16},{12,20},{16,24},{20,28},{24,0},{28,4},{1,9},{5... | collective-permute-start | bytes 884744 | tf_op jit(solution)/shard_map/ppermute | solution.py:210
  13.7 42.6 %collective-permute-start.2 = (bf16[8,144,128]{2,1,0:T(8,128)(2,1)}, bf16[8,144,128]{2,1,0:T(8,128)(2,1)}, u32[]{:S(2)}, u32[]{:S(2)}) collective-permute-start(bf16[8,144,128]{2,1,0:T(8,128)(2,1)} %bitcast.156), channel_id=1, source_target_pairs={{0,12},{4,16},{8,20},{12,24},{16,28},{20,0},{24,4},{28,8},{1,13},{... | collective-permute-start | bytes 884744 | tf_op jit(solution)/shard_map/ppermute | solution.py:210
  15.6 45.9 %collective-permute-start.3 = (bf16[8,144,128]{2,1,0:T(8,128)(2,1)}, bf16[8,144,128]{2,1,0:T(8,128)(2,1)}, u32[]{:S(2)}, u32[]{:S(2)}) collective-permute-start(bf16[8,144,128]{2,1,0:T(8,128)(2,1)} %bitcast.155), channel_id=1, source_target_pairs={{0,16},{4,20},{8,24},{12,28},{16,0},{20,4},{24,8},{28,12},{1,17},{... | collective-permute-start | bytes 884744 | tf_op jit(solution)/shard_map/ppermute | solution.py:210
  18.1 43.4 %collective-permute-start.4 = (bf16[8,144,128]{2,1,0:T(8,128)(2,1)}, bf16[8,144,128]{2,1,0:T(8,128)(2,1)}, u32[]{:S(2)}, u32[]{:S(2)}) collective-permute-start(bf16[8,144,128]{2,1,0:T(8,128)(2,1)} %bitcast.154), channel_id=1, source_target_pairs={{0,20},{4,24},{8,28},{12,0},{16,4},{20,8},{24,12},{28,16},{1,21},{... | collective-permute-start | bytes 884744 | tf_op jit(solution)/shard_map/ppermute | solution.py:210
  20.9 29.1 %copy-start.6 = (bf16[8,144,128]{2,1,0:T(8,128)(2,1)}, bf16[8,144,128]{2,1,0:T(8,128)(2,1)S(1)}, u32[]{:S(2)}) copy-start(bf16[8,144,128]{2,1,0:T(8,128)(2,1)S(1)} %collective-permute-done.refs_1_) | copy-start | bytes 884740
  20.9 42.3 %collective-permute-start.5 = (bf16[8,144,128]{2,1,0:T(8,128)(2,1)}, bf16[8,144,128]{2,1,0:T(8,128)(2,1)S(1)}, u32[]{:S(2)}, u32[]{:S(2)}) collective-permute-start(bf16[8,144,128]{2,1,0:T(8,128)(2,1)} %bitcast.153), channel_id=1, source_target_pairs={{0,24},{4,28},{8,0},{12,4},{16,8},{20,12},{24,16},{28,20},{1,25},{... | collective-permute-start | bytes 884744 | tf_op jit(solution)/shard_map/ppermute | solution.py:210
  50.0 0.7 copy-start.7
  50.0 15.1 %collective-permute-start.6 = (bf16[8,144,128]{2,1,0:T(8,128)(2,1)}, bf16[8,144,128]{2,1,0:T(8,128)(2,1)S(1)}, u32[]{:S(2)}, u32[]{:S(2)}) collective-permute-start(bf16[8,144,128]{2,1,0:T(8,128)(2,1)} %bitcast.152), channel_id=1, source_target_pairs={{0,28},{4,0},{8,4},{12,8},{16,12},{20,16},{24,20},{28,24},{1,29},{... | collective-permute-start | bytes 884744 | tf_op jit(solution)/shard_map/ppermute | solution.py:210
  50.1 24.0 %copy-start.3 = (bf16[1,8,144,128]{3,2,1,0:T(8,128)(2,1)}, bf16[1,8,144,128]{3,2,1,0:T(8,128)(2,1)S(1)}, u32[]{:S(2)}) copy-start(bf16[1,8,144,128]{3,2,1,0:T(8,128)(2,1)S(1)} %copy.255) | copy-start | bytes 884740
  63.2 5.7 %copy-start.8 = (bf16[8,144,128]{2,1,0:T(8,128)(2,1)}, bf16[8,144,128]{2,1,0:T(8,128)(2,1)S(1)}, u32[]{:S(2)}) copy-start(bf16[8,144,128]{2,1,0:T(8,128)(2,1)S(1)} %collective-permute-done.5.refs_6_) | copy-start | bytes 884740
  65.1 3.8 %copy-start.9 = (bf16[8,144,128]{2,1,0:T(8,128)(2,1)}, bf16[8,144,128]{2,1,0:T(8,128)(2,1)S(1)}, u32[]{:S(2)}) copy-start(bf16[8,144,128]{2,1,0:T(8,128)(2,1)S(1)} %collective-permute-done.6.refs_7_) | copy-start | bytes 884740
  82.9 8.5 %collective-permute-start.7 = (f32[2,1032,256]{2,1,0:T(8,128)}, f32[2,1032,256]{2,1,0:T(8,128)}, u32[]{:S(2)}, u32[]{:S(2)}) collective-permute-start(f32[2,1032,256]{2,1,0:T(8,128)} %slice.219), channel_id=1, source_target_pairs={{0,1},{1,0},{2,3},{3,2},{4,5},{5,4},{6,7},{7,6},{8,9},{9,8},{10,11... | collective-permute-start | bytes 6340616 | tf_op jit(solution)/shard_map/ppermute | solution.py:155
  86.4 35.4 %all-to-all-start = ((bf16[8,4,128,128]{3,2,1,0:T(8,128)(2,1)}), bf16[8,4,128,128]{3,2,1,0:T(8,128)(2,1)}, u32[]{:S(2)}, u32[]{:S(2)}) async-start(bf16[8,4,128,128]{3,2,1,0:T(8,128)(2,1)} %get-tuple-element.84), calls=%async_computation | async-start | bytes 2097152 | tf_op jit(solution)/shard_map/all_to_all | solution.py:250
  93.8 2.7 %copy-start.12 = (bf16[9,41]{1,0:T(8,128)(2,1)S(1)}, bf16[9,41]{1,0:T(8,128)(2,1)}, u32[]{:S(2)}) copy-start(bf16[9,41]{1,0:T(8,128)(2,1)} %param.19) | copy-start | bytes 2218
  93.8 4.1 %copy-start.5 = (bf16[128,9,128]{2,1,0:T(8,128)(2,1)S(1)}, bf16[128,9,128]{2,1,0:T(8,128)(2,1)}, u32[]{:S(2)}) copy-start(bf16[128,9,128]{2,1,0:T(8,128)(2,1)} %fusion.8) | copy-start | bytes 884740
  94.9 25.5 %collective-permute-start.8 = (f32[1,1032,256]{2,1,0:T(8,128)}, f32[1,1032,256]{2,1,0:T(8,128)}, u32[]{:S(2)}, u32[]{:S(2)}) collective-permute-start(f32[1,1032,256]{2,1,0:T(8,128)} %slice.221), channel_id=1, source_target_pairs={{0,2},{1,3},{2,0},{3,1},{4,6},{5,7},{6,4},{7,5},{8,10},{9,11},{10,... | collective-permute-start | bytes 3170312 | tf_op jit(solution)/shard_map/ppermute | solution.py:155
  121.8 30.4 %all-to-all-start.1 = ((bf16[8,4,128,128]{3,2,1,0:T(8,128)(2,1)}), bf16[8,4,128,128]{3,2,1,0:T(8,128)(2,1)S(1)}, u32[]{:S(2)}, u32[]{:S(2)}) async-start(bf16[8,4,128,128]{3,2,1,0:T(8,128)(2,1)} %get-tuple-element.30), calls=%async_computation.1 | async-start | bytes 2097152 | tf_op jit(solution)/shard_map/all_to_all | solution.py:252
  128.1 9.9 %copy-start.11 = (s32[32]{0:T(128)}, s32[32]{0:T(128)S(1)}, u32[]{:S(2)}) copy-start(s32[32]{0:T(128)S(1)} %squeeze_reshape.28.row_ref) | copy-start | bytes 388
  132.1 20.1 %copy-start.10 = (s32[32]{0:T(128)}, s32[32]{0:T(128)S(1)}, u32[]{:S(2)}) copy-start(s32[32]{0:T(128)S(1)} %squeeze_reshape.24.row_ref) | copy-start | bytes 388
  152.2 1.0 copy-start.2
  168.7 6.1 %copy-start.1 = (f32[4,1024,256]{2,1,0:T(8,128)S(1)}, f32[4,1024,256]{2,1,0:T(8,128)}, u32[]{:S(2)}) copy-start(f32[4,1024,256]{2,1,0:T(8,128)} %shard_map.96) | copy-start | bytes 12582916
  170.5 4.2 %collective-permute-start.9 = (f32[2,1024,256]{2,1,0:T(8,128)S(1)}, f32[2,1024,256]{2,1,0:T(8,128)S(1)}, u32[]{:S(2)}, u32[]{:S(2)}) collective-permute-start(f32[2,1024,256]{2,1,0:T(8,128)S(1)} %slice.226), channel_id=1, source_target_pairs={{0,1},{1,0},{2,3},{3,2},{4,5},{5,4},{6,7},{7,6},{8,9},{9,8},{10,11... | collective-permute-start | bytes 6291464 | tf_op jit(solution)/shard_map/ppermute | solution.py:155
  176.1 25.5 %collective-permute-start.10 = (f32[1,1024,256]{2,1,0:T(8,128)}, f32[1,1024,256]{2,1,0:T(8,128)}, u32[]{:S(2)}, u32[]{:S(2)}) collective-permute-start(f32[1,1024,256]{2,1,0:T(8,128)} %slice.228), channel_id=1, source_target_pairs={{0,2},{1,3},{2,0},{3,1},{4,6},{5,7},{6,4},{7,5},{8,10},{9,11},{10,... | collective-permute-start | bytes 3145736 | tf_op jit(solution)/shard_map/ppermute | solution.py:155
where the time goes:
time: 206 us; the launch traced here: 205 us
  waiting for transfers between devices  83.7 us (41%)
  local copies, waits for them, and re-layouts  35.5 us (17%)
  Pallas kernels  35.4 us (17%)
  starting transfers between devices  22.7 us (11%)
  other arithmetic  21.8 us (11%)
  matrix products  4.82 us (2%)
    ppermute x4, waiting for transfers between devices, reduce_scatter_visit(): field = field[:half] + lax.ppermute(field[half:], 'visit', perm=pairs)  42.3 us
    ppermute x7, waiting for transfers between devices, shards(): got_vm.append(lax.ppermute(send_vm[step], 'sky', perm=pairs))  41.4 us
    pallas_call x2, Pallas kernels, image_field(): pl.pallas_call(functools.partial(image_kernel, field is not None), out_sh...  29.7 us
    ppermute x7, starting transfers between devices, shards(): got_vm.append(lax.ppermute(send_vm[step], 'sky', perm=pairs))  8.49 us
    unnamed x44, local copies, waits for them, and re-layouts  8.47 us
    slice x4, local copies, waits for them, and re-layouts, reduce_scatter_visit(): field = field[:half] + lax.ppermute(field[half:], 'visit', perm=pairs)  7.05 us
    all_to_all x1, starting transfers between devices, shards(): lax.all_to_all(send_b, 'sky', split_axis=0, concat_axis=0, tiled=True)  6.01 us
    pallas_call x1, Pallas kernels, variance_field(): pl.pallas_call(variance_kernel, out_shape=jax.ShapeDtypeStruct(field_shap...  5.68 us
  transfers between devices with their start and end apart: 13, of which 8 were waited for; matrix products, arithmetic and copies ran while one was open for 16% of the time, Pallas kernels for 7%

commit v1 on v0

--- a/solution.py
+++ b/solution.py
@@ -248,8 +248,9 @@
 
     low = held_most // 2
     part_a = lax.all_to_all(send_im[:, :low], "sky", split_axis=0, concat_axis=0, tiled=True)
-    var_share, part_a, send_b = lax.optimization_barrier((var_share, part_a, send_im[:, low:]))
+    part_a, send_b = lax.optimization_barrier((part_a, send_im[:, low:]))
     part_b = lax.all_to_all(send_b, "sky", split_axis=0, concat_axis=0, tiled=True)
+    var_share, part_b = lax.optimization_barrier((var_share, part_b))
     source = (me - jnp.arange(n_sky)) % n_sky
 
     def by_source(values, lower, upper):

time: 206 us -> 199 us (0.966)
  the two profiles are of different devices: /device:TPU:10 before, /device:TPU:0 now
where the time goes in v1:
time: 199 us
  waiting for transfers between devices  66.8 us (34%)
  starting transfers between devices  42.9 us (22%)
  Pallas kernels  35.3 us (18%)
  local copies, waits for them, and re-layouts  27.7 us (14%)
  other arithmetic  22.1 us (11%)
  matrix products  3.25 us (2%)
    pallas_call x2, Pallas kernels, image_field(): pl.pallas_call(functools.partial(image_kernel, field is not None), out_sh...  29.6 us
    ppermute x4, waiting for transfers between devices, reduce_scatter_visit(): field = field[:half] + lax.ppermute(field[half:], 'visit', perm=pairs)  28.1 us
    ppermute x7, waiting for transfers between devices, shards(): got_vm.append(lax.ppermute(send_vm[step], 'sky', perm=pairs))  20.6 us
    all_to_all x1, starting transfers between devices, shards(): lax.all_to_all(send_im[:, :low], 'sky', split_axis=0, concat_axis=0, tile...  18.6 us
    all_to_all x1, waiting for transfers between devices, shards(): lax.all_to_all(send_im[:, :low], 'sky', split_axis=0, concat_axis=0, tile...  18 us
    ppermute x7, starting transfers between devices, shards(): got_vm.append(lax.ppermute(send_vm[step], 'sky', perm=pairs))  16.9 us
    slice x4, local copies, waits for them, and re-layouts, reduce_scatter_visit(): field = field[:half] + lax.ppermute(field[half:], 'visit', perm=pairs)  6.07 us
    pallas_call x1, Pallas kernels, variance_field(): pl.pallas_call(variance_kernel, out_shape=jax.ShapeDtypeStruct(field_shap...  5.68 us
  transfers between devices with their start and end apart: 13, of which 7 were waited for; matrix products, arithmetic and copies ran while one was open for 14% of the time, Pallas kernels for 7%

profile of v1, /device:TPU:0, one launch (start us, length us, event | category | flops | bytes accessed | tf_op | source)
XLA Modules:
  0.0 199.2 jit_solution(13319634105594004601)
XLA Ops:
  0.6 1.6 convert_reduce_fusion
  5.9 1.5 maximum_maximum_fusion
  9.1 2.9 %collective-permute-start = (bf16[8,144,128]{2,1,0:T(8,128)(2,1)}, bf16[8,144,128]{2,1,0:T(8,128)(2,1)S(1)}, u32[]{:S(2)}, u32[]{:S(2)}) collective-permute-start(bf16[8,144,128]{2,1,0:T(8,128)(2,1)} %bitcast.158), channel_id=1, source_target_pairs={{0,4},{4,8},{8,12},{12,16},{16,20},{20,24},{24,28},{28,0},{1,5},{5... | collective-permute-start | bytes 884744 | tf_op jit(solution)/shard_map/ppermute | solution.py:210
  12.8 1.6 collective-permute-start.1
  15.1 2.6 %collective-permute-start.2 = (bf16[8,144,128]{2,1,0:T(8,128)(2,1)}, bf16[8,144,128]{2,1,0:T(8,128)(2,1)S(1)}, u32[]{:S(2)}, u32[]{:S(2)}) collective-permute-start(bf16[8,144,128]{2,1,0:T(8,128)(2,1)} %bitcast.156), channel_id=1, source_target_pairs={{0,12},{4,16},{8,20},{12,24},{16,28},{20,0},{24,4},{28,8},{1,13},{... | collective-permute-start | bytes 884744 | tf_op jit(solution)/shard_map/ppermute | solution.py:210
  18.4 1.2 collective-permute-start.3
  20.4 2.6 %collective-permute-start.4 = (bf16[8,144,128]{2,1,0:T(8,128)(2,1)}, bf16[8,144,128]{2,1,0:T(8,128)(2,1)}, u32[]{:S(2)}, u32[]{:S(2)}) collective-permute-start(bf16[8,144,128]{2,1,0:T(8,128)(2,1)} %bitcast.154), channel_id=1, source_target_pairs={{0,20},{4,24},{8,28},{12,0},{16,4},{20,8},{24,12},{28,16},{1,21},{... | collective-permute-start | bytes 884744 | tf_op jit(solution)/shard_map/ppermute | solution.py:210
  24.8 1.4 collective-permute-start.5
  26.2 4.6 %collective-permute-start.6 = (bf16[8,144,128]{2,1,0:T(8,128)(2,1)S(1)}, bf16[8,144,128]{2,1,0:T(8,128)(2,1)S(1)}, u32[]{:S(2)}, u32[]{:S(2)}) collective-permute-start(bf16[8,144,128]{2,1,0:T(8,128)(2,1)S(1)} %bitcast.169), channel_id=1, source_target_pairs={{0,28},{4,0},{8,4},{12,8},{16,12},{20,16},{24,20},{28,24},{1,29},{... | collective-permute-start | bytes 884744 | tf_op jit(solution)/shard_map/ppermute | solution.py:210
  31.6 16.1 %collective-permute-done.2.refs_3_ = bf16[8,144,128]{2,1,0:T(8,128)(2,1)S(1)} collective-permute-done((bf16[8,144,128]{2,1,0:T(8,128)(2,1)}, bf16[8,144,128]{2,1,0:T(8,128)(2,1)S(1)}, u32[]{:S(2)}, u32[]{:S(2)}) %collective-permute-start.2) | collective-permute-done | bytes 294944 | tf_op jit(solution)/shard_map/ppermute | solution.py:210
  47.7 1.0 collective-permute-done.3.refs_4_
  48.8 3.4 %collective-permute-done.6.refs_7_ = bf16[8,144,128]{2,1,0:T(8,128)(2,1)S(1)} collective-permute-done((bf16[8,144,128]{2,1,0:T(8,128)(2,1)S(1)}, bf16[8,144,128]{2,1,0:T(8,128)(2,1)S(1)}, u32[]{:S(2)}, u32[]{:S(2)}) %collective-permute-start.6) | collective-permute-done | bytes 294944 | tf_op jit(solution)/shard_map/ppermute | solution.py:210
  59.0 5.7 %shard_map.94 = f32[4,1032,256]{2,1,0:T(8,128)} custom-call(s32[64]{0:T(128)} %get-tuple-element.107.row_ref, s32[64]{0:T(128)} %get-tuple-element.106.group_ref, s32[64]{0:T(128)} %get-tuple-element.72.sub_ref, f32[64]{0:T(128)} %mul.32.w2_ref, bf16[8,144,128]{2,1,0:T(8,128)(2,1)} %bitcast.164, bf16[8,144,128]{2,1,0:T(8,128)(2,1)} %copy-done.5, ...), custom_call_target="tpu_custom_call" | custom-call | tf_op jit(solution)/shard_map/pallas_call | solution.py:106
  64.7 3.1 %slice.219 = f32[2,1032,256]{2,1,0:T(8,128)} slice(f32[4,1032,256]{2,1,0:T(8,128)} %shard_map.94), slice={[2:4], [0:1032], [0:256]} | slice | bytes 4227072 | tf_op jit(solution)/shard_map/slice | solution.py:155
  67.8 1.5 fusion.54
  69.2 18.6 %all-to-all-start = ((bf16[8,4,128,128]{3,2,1,0:T(8,128)(2,1)}), bf16[8,4,128,128]{3,2,1,0:T(8,128)(2,1)S(1)}, u32[]{:S(2)}, u32[]{:S(2)}) async-start(bf16[8,4,128,128]{3,2,1,0:T(8,128)(2,1)} %get-tuple-element.86), calls=%async_computation | async-start | bytes 2097152 | tf_op jit(solution)/shard_map/all_to_all | solution.py:250
  96.2 18.0 %all-to-all-done = bf16[8,4,128,128]{3,2,1,0:T(8,128)(2,1)S(1)} async-done(((bf16[8,4,128,128]{3,2,1,0:T(8,128)(2,1)}), bf16[8,4,128,128]{3,2,1,0:T(8,128)(2,1)S(1)}, u32[]{:S(2)}, u32[]{:S(2)}) %all-to-all-start) | async-done | bytes 1048608 | tf_op jit(solution)/shard_map/all_to_all | solution.py:250
  114.2 4.2 %all-to-all-start.1 = ((bf16[8,4,128,128]{3,2,1,0:T(8,128)(2,1)}), bf16[8,4,128,128]{3,2,1,0:T(8,128)(2,1)}, u32[]{:S(2)}, u32[]{:S(2)}) async-start(bf16[8,4,128,128]{3,2,1,0:T(8,128)(2,1)} %get-tuple-element.31), calls=%async_computation.1 | async-start | bytes 2097152 | tf_op jit(solution)/shard_map/all_to_all | solution.py:252
  118.5 2.5 %slice_add_fusion = f32[2,1032,256]{2,1,0:T(8,128)S(1)} fusion(f32[2,1032,256]{2,1,0:T(8,128)} %collective-permute-done.7, f32[4,1032,256]{2,1,0:T(8,128)} %shard_map.94), kind=kLoop, calls=%fused_computation.11 | loop fusion | flops 528384 | bytes 6340608 | tf_op jit(solution)/shard_map/add | solution.py:155
  121.1 1.6 collective-permute-start.8
  126.1 1.7 sort.32
  127.8 1.7 sort.31
  129.5 14.2 %shard_map.95.refs_0_ = f32[4,1024,256]{2,1,0:T(8,128)} custom-call(s32[32]{0:T(128)} %get-tuple-element.33.order_ref, s32[1]{0:T(128)} %bitcast.29.count_ref, s32[32]{0:T(128)} %copy-done.12, s32[32]{0:T(128)} %squeeze_reshape.29.group_ref, s32[32]{0:T(128)} %squeeze_reshape.30.sub_ref, f32[32]{0:T(128)} %squeeze_reshape.31.w_ref, ...), custom_call_target="tpu_custom_call" | custom-call | flops 2415919104 | bytes 9437184 | tf_op jit(solution)/shard_map/pallas_call | solution.py:121
  143.7 2.2 %collective-permute-done.8 = f32[1,1032,256]{2,1,0:T(8,128)} collective-permute-done((f32[1,1032,256]{2,1,0:T(8,128)S(1)}, f32[1,1032,256]{2,1,0:T(8,128)}, u32[]{:S(2)}, u32[]{:S(2)}) %collective-permute-start.8) | collective-permute-done | bytes 1056800 | tf_op jit(solution)/shard_map/ppermute | solution.py:155
  145.9 1.4 fusion.11
  147.3 15.5 %shard_map.96 = f32[4,1024,256]{2,1,0:T(8,128)} custom-call(s32[32]{0:T(128)} %get-tuple-element.29.order_ref, s32[1]{0:T(128)} %bitcast.9.count_ref, s32[32]{0:T(128)} %copy-done.11, s32[32]{0:T(128)} %squeeze_reshape.25.group_ref, s32[32]{0:T(128)} %squeeze_reshape.26.sub_ref, f32[32]{0:T(128)} %squeeze_reshape.27.w_ref, ...), custom_call_target="tpu_custom_call", output_to_operand_aliasing={{}: (10, {})} | custom-call | flops 2415919104 | bytes 9437184 | tf_op jit(solution)/shard_map/pallas_call | solution.py:121
  162.8 1.9 slice.226
  164.8 4.1 %collective-permute-done.9 = f32[2,1024,256]{2,1,0:T(8,128)S(1)} collective-permute-done((f32[2,1024,256]{2,1,0:T(8,128)S(1)}, f32[2,1024,256]{2,1,0:T(8,128)S(1)}, u32[]{:S(2)}, u32[]{:S(2)}) %collective-permute-start.9) | collective-permute-done | bytes 2097184 | tf_op jit(solution)/shard_map/ppermute | solution.py:155
  169.2 1.0 slice.228
  170.3 1.5 collective-permute-start.10
  174.0 21.7 %collective-permute-done.10 = f32[1,1024,256]{2,1,0:T(8,128)} collective-permute-done((f32[1,1024,256]{2,1,0:T(8,128)}, f32[1,1024,256]{2,1,0:T(8,128)}, u32[]{:S(2)}, u32[]{:S(2)}) %collective-permute-start.10) | collective-permute-done | bytes 1048608 | tf_op jit(solution)/shard_map/ppermute | solution.py:155
  196.1 3.1 %fusion.12 = (f32[1024,256]{1,0:T(8,128)}, f32[1024,256]{1,0:T(8,128)}) fusion(f32[1032,256]{1,0:T(8,128)S(1)} %fusion.11, f32[128,8,2,128]{3,2,1,0:T(2,128)S(1)} %bitcast.162, f32[1,1024,256]{2,1,0:T(8,128)} %collective-permute-done.10, f32[2,1024,256]{2,1,0:T(8,128)S(1)} %slice_add_fusion.1), kind=kLoop, calls=%fused_computation.29 | loop fusion | flops 1048576 | bytes 6291456 | tf_op jit(solution)/shard_map/div | solution.py:278
  (152 shorter events, 32.3 us)
Async XLA Ops:
  0.6 23.4 %copy-start = (bf16[9,41]{1,0:T(8,128)(2,1)S(1)}, bf16[9,41]{1,0:T(8,128)(2,1)}, u32[]{:S(2)}) copy-start(bf16[9,41]{1,0:T(8,128)(2,1)} %param.18) | copy-start | bytes 2218
  8.3 14.7 %copy-start.3 = (bf16[1,32,128,128]{3,2,1,0:T(8,128)(2,1)S(1)}, bf16[1,32,128,128]{3,2,1,0:T(8,128)(2,1)}, u32[]{:S(2)}) copy-start(bf16[1,32,128,128]{3,2,1,0:T(8,128)(2,1)} %param.13) | copy-start | bytes 3145732
  9.1 15.6 %collective-permute-start = (bf16[8,144,128]{2,1,0:T(8,128)(2,1)}, bf16[8,144,128]{2,1,0:T(8,128)(2,1)S(1)}, u32[]{:S(2)}, u32[]{:S(2)}) collective-permute-start(bf16[8,144,128]{2,1,0:T(8,128)(2,1)} %bitcast.158), channel_id=1, source_target_pairs={{0,4},{4,8},{8,12},{12,16},{16,20},{20,24},{24,28},{28,0},{1,5},{5... | collective-permute-start | bytes 884744 | tf_op jit(solution)/shard_map/ppermute | solution.py:210
  12.8 13.4 %collective-permute-start.1 = (bf16[8,144,128]{2,1,0:T(8,128)(2,1)}, bf16[8,144,128]{2,1,0:T(8,128)(2,1)S(1)}, u32[]{:S(2)}, u32[]{:S(2)}) collective-permute-start(bf16[8,144,128]{2,1,0:T(8,128)(2,1)} %bitcast.157), channel_id=1, source_target_pairs={{0,8},{4,12},{8,16},{12,20},{16,24},{20,28},{24,0},{28,4},{1,9},{5... | collective-permute-start | bytes 884744 | tf_op jit(solution)/shard_map/ppermute | solution.py:210
  15.1 32.6 %collective-permute-start.2 = (bf16[8,144,128]{2,1,0:T(8,128)(2,1)}, bf16[8,144,128]{2,1,0:T(8,128)(2,1)S(1)}, u32[]{:S(2)}, u32[]{:S(2)}) collective-permute-start(bf16[8,144,128]{2,1,0:T(8,128)(2,1)} %bitcast.156), channel_id=1, source_target_pairs={{0,12},{4,16},{8,20},{12,24},{16,28},{20,0},{24,4},{28,8},{1,13},{... | collective-permute-start | bytes 884744 | tf_op jit(solution)/shard_map/ppermute | solution.py:210
  18.4 30.3 %collective-permute-start.3 = (bf16[8,144,128]{2,1,0:T(8,128)(2,1)}, bf16[8,144,128]{2,1,0:T(8,128)(2,1)S(1)}, u32[]{:S(2)}, u32[]{:S(2)}) collective-permute-start(bf16[8,144,128]{2,1,0:T(8,128)(2,1)} %bitcast.155), channel_id=1, source_target_pairs={{0,16},{4,20},{8,24},{12,28},{16,0},{20,4},{24,8},{28,12},{1,17},{... | collective-permute-start | bytes 884744 | tf_op jit(solution)/shard_map/ppermute | solution.py:210
  20.4 28.3 %collective-permute-start.4 = (bf16[8,144,128]{2,1,0:T(8,128)(2,1)}, bf16[8,144,128]{2,1,0:T(8,128)(2,1)}, u32[]{:S(2)}, u32[]{:S(2)}) collective-permute-start(bf16[8,144,128]{2,1,0:T(8,128)(2,1)} %bitcast.154), channel_id=1, source_target_pairs={{0,20},{4,24},{8,28},{12,0},{16,4},{20,8},{24,12},{28,16},{1,21},{... | collective-permute-start | bytes 884744 | tf_op jit(solution)/shard_map/ppermute | solution.py:210
  23.9 7.0 %copy-start.13 = (bf16[9,41]{1,0:T(8,128)(2,1)S(1)}, bf16[9,41]{1,0:T(8,128)(2,1)}, u32[]{:S(2)}) copy-start(bf16[9,41]{1,0:T(8,128)(2,1)} %param.19) | copy-start | bytes 2218
  24.8 30.1 %copy-start.5 = (bf16[8,144,128]{2,1,0:T(8,128)(2,1)}, bf16[8,144,128]{2,1,0:T(8,128)(2,1)S(1)}, u32[]{:S(2)}) copy-start(bf16[8,144,128]{2,1,0:T(8,128)(2,1)S(1)} %collective-permute-done.refs_1_) | copy-start | bytes 884740
  24.8 24.0 %collective-permute-start.5 = (bf16[8,144,128]{2,1,0:T(8,128)(2,1)S(1)}, bf16[8,144,128]{2,1,0:T(8,128)(2,1)S(1)}, u32[]{:S(2)}, u32[]{:S(2)}) collective-permute-start(bf16[8,144,128]{2,1,0:T(8,128)(2,1)S(1)} %bitcast.170), channel_id=1, source_target_pairs={{0,24},{4,28},{8,0},{12,4},{16,8},{20,12},{24,16},{28,20},{1,25},{... | collective-permute-start | bytes 884744 | tf_op jit(solution)/shard_map/ppermute | solution.py:210
  26.2 28.7 %copy-start.6 = (bf16[8,144,128]{2,1,0:T(8,128)(2,1)}, bf16[8,144,128]{2,1,0:T(8,128)(2,1)S(1)}, u32[]{:S(2)}) copy-start(bf16[8,144,128]{2,1,0:T(8,128)(2,1)S(1)} %collective-permute-done.1.refs_2_) | copy-start | bytes 884740
  26.2 26.0 %collective-permute-start.6 = (bf16[8,144,128]{2,1,0:T(8,128)(2,1)S(1)}, bf16[8,144,128]{2,1,0:T(8,128)(2,1)S(1)}, u32[]{:S(2)}, u32[]{:S(2)}) collective-permute-start(bf16[8,144,128]{2,1,0:T(8,128)(2,1)S(1)} %bitcast.169), channel_id=1, source_target_pairs={{0,28},{4,0},{8,4},{12,8},{16,12},{20,16},{24,20},{28,24},{1,29},{... | collective-permute-start | bytes 884744 | tf_op jit(solution)/shard_map/ppermute | solution.py:210
  30.8 25.2 %copy-start.2 = (bf16[1,8,144,128]{3,2,1,0:T(8,128)(2,1)}, bf16[1,8,144,128]{3,2,1,0:T(8,128)(2,1)S(1)}, u32[]{:S(2)}) copy-start(bf16[1,8,144,128]{3,2,1,0:T(8,128)(2,1)S(1)} %copy.255) | copy-start | bytes 884740
  47.7 7.1 %copy-start.7 = (bf16[8,144,128]{2,1,0:T(8,128)(2,1)}, bf16[8,144,128]{2,1,0:T(8,128)(2,1)S(1)}, u32[]{:S(2)}) copy-start(bf16[8,144,128]{2,1,0:T(8,128)(2,1)S(1)} %collective-permute-done.2.refs_3_) | copy-start | bytes 884740
  48.8 6.1 %copy-start.8 = (bf16[8,144,128]{2,1,0:T(8,128)(2,1)}, bf16[8,144,128]{2,1,0:T(8,128)(2,1)S(1)}, u32[]{:S(2)}) copy-start(bf16[8,144,128]{2,1,0:T(8,128)(2,1)S(1)} %collective-permute-done.3.refs_4_) | copy-start | bytes 884740
  48.8 6.1 %copy-start.9 = (bf16[8,144,128]{2,1,0:T(8,128)(2,1)}, bf16[8,144,128]{2,1,0:T(8,128)(2,1)S(1)}, u32[]{:S(2)}) copy-start(bf16[8,144,128]{2,1,0:T(8,128)(2,1)S(1)} %collective-permute-done.5.refs_6_) | copy-start | bytes 884740
  52.2 2.7 %copy-start.10 = (bf16[8,144,128]{2,1,0:T(8,128)(2,1)}, bf16[8,144,128]{2,1,0:T(8,128)(2,1)S(1)}, u32[]{:S(2)}) copy-start(bf16[8,144,128]{2,1,0:T(8,128)(2,1)S(1)} %collective-permute-done.6.refs_7_) | copy-start | bytes 884740
  67.8 50.7 %collective-permute-start.7 = (f32[2,1032,256]{2,1,0:T(8,128)}, f32[2,1032,256]{2,1,0:T(8,128)}, u32[]{:S(2)}, u32[]{:S(2)}) collective-permute-start(f32[2,1032,256]{2,1,0:T(8,128)} %slice.219), channel_id=1, source_target_pairs={{0,1},{1,0},{2,3},{3,2},{4,5},{5,4},{6,7},{7,6},{8,9},{9,8},{10,11... | collective-permute-start | bytes 6340616 | tf_op jit(solution)/shard_map/ppermute | solution.py:155
  69.2 45.0 %all-to-all-start = ((bf16[8,4,128,128]{3,2,1,0:T(8,128)(2,1)}), bf16[8,4,128,128]{3,2,1,0:T(8,128)(2,1)S(1)}, u32[]{:S(2)}, u32[]{:S(2)}) async-start(bf16[8,4,128,128]{3,2,1,0:T(8,128)(2,1)} %get-tuple-element.86), calls=%async_computation | async-start | bytes 2097152 | tf_op jit(solution)/shard_map/all_to_all | solution.py:250
  92.8 33.3 %copy-start.12 = (s32[32]{0:T(128)}, s32[32]{0:T(128)S(1)}, u32[]{:S(2)}) copy-start(s32[32]{0:T(128)S(1)} %squeeze_reshape.28.row_ref) | copy-start | bytes 388
  114.2 4.3 %copy-start.4 = (bf16[8,4,128,128]{3,2,1,0:T(8,128)(2,1)}, bf16[8,4,128,128]{3,2,1,0:T(8,128)(2,1)S(1)}, u32[]{:S(2)}) copy-start(bf16[8,4,128,128]{3,2,1,0:T(8,128)(2,1)S(1)} %all-to-all-done) | copy-start | bytes 3145732
  114.2 33.1 %all-to-all-start.1 = ((bf16[8,4,128,128]{3,2,1,0:T(8,128)(2,1)}), bf16[8,4,128,128]{3,2,1,0:T(8,128)(2,1)}, u32[]{:S(2)}, u32[]{:S(2)}) async-start(bf16[8,4,128,128]{3,2,1,0:T(8,128)(2,1)} %get-tuple-element.31), calls=%async_computation.1 | async-start | bytes 2097152 | tf_op jit(solution)/shard_map/all_to_all | solution.py:252
  121.1 24.8 %collective-permute-start.8 = (f32[1,1032,256]{2,1,0:T(8,128)S(1)}, f32[1,1032,256]{2,1,0:T(8,128)}, u32[]{:S(2)}, u32[]{:S(2)}) collective-permute-start(f32[1,1032,256]{2,1,0:T(8,128)S(1)} %slice.221), channel_id=1, source_target_pairs={{0,2},{1,3},{2,0},{3,1},{4,6},{5,7},{6,4},{7,5},{8,10},{9,11},{10,... | collective-permute-start | bytes 3170312 | tf_op jit(solution)/shard_map/ppermute | solution.py:155
  123.5 20.1 %copy-start.11 = (s32[32]{0:T(128)}, s32[32]{0:T(128)S(1)}, u32[]{:S(2)}) copy-start(s32[32]{0:T(128)S(1)} %squeeze_reshape.24.row_ref) | copy-start | bytes 388
  162.8 6.1 %copy-start.1 = (f32[4,1024,256]{2,1,0:T(8,128)S(1)}, f32[4,1024,256]{2,1,0:T(8,128)}, u32[]{:S(2)}) copy-start(f32[4,1024,256]{2,1,0:T(8,128)} %shard_map.96) | copy-start | bytes 12582916
  164.7 4.2 %collective-permute-start.9 = (f32[2,1024,256]{2,1,0:T(8,128)S(1)}, f32[2,1024,256]{2,1,0:T(8,128)S(1)}, u32[]{:S(2)}, u32[]{:S(2)}) collective-permute-start(f32[2,1024,256]{2,1,0:T(8,128)S(1)} %slice.226), channel_id=1, source_target_pairs={{0,1},{1,0},{2,3},{3,2},{4,5},{5,4},{6,7},{7,6},{8,9},{9,8},{10,11... | collective-permute-start | bytes 6291464 | tf_op jit(solution)/shard_map/ppermute | solution.py:155
  170.3 25.5 %collective-permute-start.10 = (f32[1,1024,256]{2,1,0:T(8,128)}, f32[1,1024,256]{2,1,0:T(8,128)}, u32[]{:S(2)}, u32[]{:S(2)}) collective-permute-start(f32[1,1024,256]{2,1,0:T(8,128)} %slice.228), channel_id=1, source_target_pairs={{0,2},{1,3},{2,0},{3,1},{4,6},{5,7},{6,4},{7,5},{8,10},{9,11},{10,... | collective-permute-start | bytes 3145736 | tf_op jit(solution)/shard_map/ppermute | solution.py:155
